TPU v7x, 256 devices: a whole 4x4x8 slice. The times are simulated.
256 devices in a mesh: req: 32 (over z, x), tp: 8 (over y, core).
Axes of the slice: x: 4, y: 4, z: 8, core: 2. Of those that a mesh axis runs over, the one named last changes fastest.
Arguments:
- hidden: bfloat16 [8192, 2048], P('req'), may hold values from -6 to 6
- kv_cache: bfloat16 [2, 1024, 128, 2048], P(None, 'req', None, 'tp'), may hold values from -64 to 64
- page_table: int32 [128, 8], P('req'), may hold values from 0 to 31, as said below
- cache_lens: int32 [128], P('req'), may hold values from 1 to 1024
- parents: int32 [128, 64], P('req'), may hold values from 0 to 62, as said below
- accepted: int32 [128, 8], P('req'), may hold values from 0 to 14, as said below
- attn_gain: float32 [2048], replicated, may hold values from 0.1 to 1.9
- w_qkv: bfloat16 [2048, 3, 2048], P(None, None, 'tp'), may hold values from -0.125 to 0.125
- qk_gain: float32 [2, 2048], P(None, 'tp'), may hold values from 0.5 to 8
- w_out: bfloat16 [2048, 2048], P('tp'), may hold values from -0.5 to 0.5
- moe_gain: float32 [2048], replicated, may hold values from 0.1 to 1.9
- routes: int32 [8192, 8], P('req'), may hold values from 0 to 63, all different within a row; in each aligned block of 256 rows (0 to 255, 256 to 511, ...) at most 40 rows name the same one
- route_weights: float32 [8192, 8], P('req'), may hold values from 0.1 to 1
- w_gate_up: bfloat16 [32, 2048, 2, 2048], P('req', None, None, 'tp'), may hold values from -0.125 to 0.125
- w_down: bfloat16 [32, 2048, 2048], P('req', 'tp'), may hold values from -0.1875 to 0.1875
Outputs:
- output: bfloat16 [8192, 2048], P('req', 'tp')
- accepted_kv: bfloat16 [2, 1024, 2048], P(None, 'req', 'tp')
Inputs may be any that keep to these rules, and one draw needn't show every extreme that they name: `page_table`: values lie in the block of 32 pages of the request's group of 4 requests; within a group every page is used once. parents[r, 0] = 0 and parents[r, j] < j for j >= 1. accepted[r] are the first 8 slots, from the root down, of a path in request r's tree. `routes`: in each aligned block of 256 rows (the tokens of one index of req), no expert is named by more than 40 rows.
All inputs are finite; a program needn't handle non-finite values.
Results may differ from a plain program's by a relative error of at most 0.012.
The roundings to bfloat16 on the way count: a program that leaves them out, or rounds other values in their place, can miss the bound.
Values may be sent and summed in bfloat16 or wider, within the bound.
No kernel may reach another device: no remote copies, remote signals or barrier semaphores. Data moves between devices by JAX's collectives and lax.ppermute only.
A program may use at most 128 MiB of HBM per device.

v0:
```python
import jax
import jax.numpy as jnp
from jax import lax
from jax.sharding import Mesh, PartitionSpec as P

HD = 128
FFE = 1024
EXPERTS = 64
CAP = 40
TP = ("th", "tl", "tc")


norm_eps = 1e-05
rope_base = 10000.0
masked_score = -1e30


def rms_scale(values, gain):
    return values * lax.rsqrt(jnp.mean(values * values, axis=-1, keepdims=True) + norm_eps) * gain


def tree_masks(parents):
    slot_count = parents.shape[-1]
    slot_ids = jnp.arange(slot_count, dtype=jnp.int32)
    parent_hot = (parents[..., :, None] == slot_ids).astype(jnp.float32)
    ancestry = jnp.minimum(jnp.eye(slot_count, dtype=jnp.float32) + parent_hot, 1.0)
    for squaring in range(slot_count.bit_length()):
        ancestry = jnp.minimum(
            jnp.einsum("rij,rjk->rik", ancestry, ancestry, precision=lax.Precision.HIGHEST), 1.0
        )
    depths = jnp.sum(ancestry, axis=-1).astype(jnp.int32) - 1
    return (ancestry, depths)


def rotate(values, positions):
    head_dim = values.shape[-1]
    half_dim = head_dim // 2
    frequency = rope_base ** (-jnp.arange(half_dim, dtype=jnp.float32) * 2.0 / head_dim)
    angles = positions.astype(jnp.float32)[:, None] * frequency[None, :]
    cosine = jnp.cos(angles)[:, None, :]
    sine_part = jnp.sin(angles)[:, None, :]
    first_half = values[..., :half_dim]
    second = values[..., half_dim:]
    return jnp.concatenate(
        [first_half * cosine - second * sine_part, second * cosine + first_half * sine_part],
        axis=-1,
    )


def local(
    hidden,
    kv_cache,
    page_table,
    cache_lens,
    parents,
    accepted,
    attn_gain,
    w_qkv,
    qk_gain,
    w_out,
    moe_gain,
    routes,
    route_weights,
    w_gate_up,
    w_down,
):
    tok_rows, model_width = hidden.shape
    th = lax.axis_index("th")
    tl = lax.axis_index("tl")
    tc = lax.axis_index("tc")
    tp_count = lax.axis_size(TP)
    req_count = lax.axis_size("req")
    slice_width = model_width // tp_count
    slice_start = ((th * lax.axis_size("tl") + tl) * lax.axis_size("tc") + tc) * slice_width
    req_local, draft_len = parents.shape
    feat_dev = w_qkv.shape[2]
    local_heads = feat_dev // HD
    ancestry, depths = tree_masks(parents)
    positions = (cache_lens[:, None] + depths).reshape(-1)
    normed_in = rms_scale(hidden.astype(jnp.float32), attn_gain).astype(jnp.bfloat16)
    projected = jnp.einsum(
        "tw,wgf->tgf", normed_in, w_qkv, preferred_element_type=jnp.float32
    )
    query_raw = projected[:, 0]
    key_raw = projected[:, 1]
    values_new = projected[:, 2].astype(jnp.bfloat16)
    swap = [(0, 1), (1, 0)]
    squares = jnp.stack(
        [jnp.sum(query_raw * query_raw, axis=-1), jnp.sum(key_raw * key_raw, axis=-1)]
    )
    squares = squares + lax.ppermute(squares, "tc", swap)
    squares = squares + lax.ppermute(squares, "tl", swap)
    squares = squares + lax.ppermute(squares, "th", swap)
    query_normed = query_raw * lax.rsqrt(squares[0][:, None] / model_width + norm_eps) * qk_gain[0]
    key_normed = key_raw * lax.rsqrt(squares[1][:, None] / model_width + norm_eps) * qk_gain[1]
    query_rot = rotate(query_normed.reshape(tok_rows, local_heads, HD), positions).astype(
        jnp.bfloat16
    )
    keys_new = rotate(key_normed.reshape(tok_rows, local_heads, HD), positions).astype(jnp.bfloat16)
    local_pages, page_len = kv_cache.shape[1], kv_cache.shape[2]
    all_keys = kv_cache[0].reshape(local_pages * page_len, feat_dev)
    all_values = kv_cache[1].reshape(local_pages * page_len, feat_dev)
    page_ids = jnp.arange(local_pages, dtype=jnp.int32)
    page_match = (page_table[:, :, None] == page_ids[None, None, :]).astype(jnp.int32)
    page_owned = jnp.sum(page_match, axis=1)
    page_start = jnp.sum(
        page_match * (jnp.arange(page_table.shape[1], dtype=jnp.int32) * page_len)[None, :, None],
        axis=1,
    )
    key_pos = (page_start[:, :, None] + jnp.arange(page_len, dtype=jnp.int32)[None, None, :]).reshape(
        req_local, local_pages * page_len
    )
    live_keys = (jnp.repeat(page_owned, page_len, axis=1) > 0) & (key_pos < cache_lens[:, None])
    score_scale = HD ** (-0.5)
    head_outputs = []
    for head in range(local_heads):
        lanes = slice(head * HD, (head + 1) * HD)
        queries = query_rot[:, head].reshape(req_local, draft_len, HD)
        own_keys = keys_new[:, head].reshape(req_local, draft_len, HD)
        own_values = values_new[:, lanes].reshape(req_local, draft_len, HD)
        cache_scores = (
            jnp.einsum(
                "rjd,cd->rjc", queries, all_keys[:, lanes], preferred_element_type=jnp.float32
            )
            * score_scale
        )
        cache_scores = jnp.where(live_keys[:, None, :], cache_scores, masked_score)
        draft_scores = (
            jnp.einsum("rjd,rid->rji", queries, own_keys, preferred_element_type=jnp.float32)
            * score_scale
        )
        draft_scores = jnp.where(ancestry > 0.5, draft_scores, masked_score)
        row_max = jnp.maximum(
            jnp.max(cache_scores, axis=-1, keepdims=True),
            jnp.max(draft_scores, axis=-1, keepdims=True),
        )
        cache_weights = jnp.exp(cache_scores - row_max)
        draft_weights = jnp.exp(draft_scores - row_max)
        total = jnp.sum(cache_weights, axis=-1, keepdims=True) + jnp.sum(
            draft_weights, axis=-1, keepdims=True
        )
        cache_probs = (cache_weights / total).astype(jnp.bfloat16)
        draft_probs = (draft_weights / total).astype(jnp.bfloat16)
        mixed = jnp.einsum(
            "rjc,cd->rjd", cache_probs, all_values[:, lanes], preferred_element_type=jnp.float32
        ) + jnp.einsum("rji,rid->rjd", draft_probs, own_values, preferred_element_type=jnp.float32)
        head_outputs.append(mixed.astype(jnp.bfloat16).reshape(tok_rows, HD))
    attn_heads = jnp.concatenate(head_outputs, axis=1)
    attn_term = jnp.dot(attn_heads, w_out, preferred_element_type=jnp.float32)
    column_groups = model_width // (2 * slice_width)
    attn_blocks = attn_term.reshape(tok_rows, column_groups, 2, slice_width)
    kept = lax.dynamic_index_in_dim(attn_blocks, tc, axis=2, keepdims=False)
    given = lax.dynamic_index_in_dim(attn_blocks, 1 - tc, axis=2, keepdims=False)
    chip_sum = kept + lax.ppermute(given, "tc", swap)
    hidden_blocks = hidden.astype(jnp.float32).reshape(tok_rows, column_groups, 2, slice_width)
    pair_blocks = chip_sum.reshape(tok_rows, column_groups // 2, 2, slice_width)
    row_sum = lax.dynamic_index_in_dim(pair_blocks, tl, axis=2, keepdims=False) + lax.ppermute(
        lax.dynamic_index_in_dim(pair_blocks, 1 - tl, axis=2, keepdims=False), "tl", swap
    )
    block_sum = lax.dynamic_index_in_dim(row_sum, th, axis=1, keepdims=False) + lax.ppermute(
        lax.dynamic_index_in_dim(row_sum, 1 - th, axis=1, keepdims=False), "th", swap
    )
    block_other = lax.ppermute(block_sum, "th", swap)
    row_sum = jnp.where(
        th == 0,
        jnp.stack([block_sum, block_other], axis=1),
        jnp.stack([block_other, block_sum], axis=1),
    )
    row_other = lax.ppermute(row_sum, "tl", swap)
    full_sum = jnp.where(
        tl == 0,
        jnp.stack([row_sum, row_other], axis=2),
        jnp.stack([row_other, row_sum], axis=2),
    ).reshape(tok_rows, column_groups, slice_width)
    residual = lax.dynamic_index_in_dim(hidden_blocks, tc, axis=2, keepdims=False) + full_sum
    own_squares = jnp.sum(residual * residual, axis=(1, 2))
    all_squares = own_squares + lax.ppermute(own_squares, "tc", swap)
    gain_here = lax.dynamic_index_in_dim(
        moe_gain.reshape(column_groups, 2, slice_width), tc, axis=1, keepdims=False
    )
    normed_half = (
        residual * lax.rsqrt(all_squares / model_width + norm_eps)[:, None, None] * gain_here
    ).astype(jnp.bfloat16).reshape(tok_rows, column_groups * slice_width)
    residual_share = lax.dynamic_index_in_dim(
        residual, th * lax.axis_size("tl") + tl, axis=1, keepdims=False
    )
    experts_here = EXPERTS // req_count
    units_dev = w_down.shape[1]
    tok_ids = jnp.arange(tok_rows, dtype=jnp.int32)
    route_hot = (routes[:, :, None] == jnp.arange(EXPERTS, dtype=jnp.int32)).astype(jnp.float32)
    per_token = jnp.sum(route_hot, axis=1)
    weight_of = jnp.sum(route_weights[:, :, None] * route_hot, axis=1)
    earlier = (tok_ids[:, None] > tok_ids[None, :]).astype(jnp.bfloat16)
    slot_of = jnp.dot(earlier, per_token.astype(jnp.bfloat16), preferred_element_type=jnp.float32)
    capacity = CAP
    cap_ids = jnp.arange(capacity, dtype=jnp.float32)
    picked_here = lax.dynamic_index_in_dim(
        per_token.reshape(tok_rows, req_count, experts_here), th, axis=2, keepdims=False
    ).T
    slot_here = lax.dynamic_index_in_dim(
        slot_of.reshape(tok_rows, req_count, experts_here), th, axis=2, keepdims=False
    ).T
    select = jnp.where(
        (picked_here[:, None, :] > 0.5) & (slot_here[:, None, :] == cap_ids[None, :, None]), 1.0, 0.0
    ).astype(jnp.bfloat16)
    send_rows = jnp.einsum(
        "ict,tw->icw", select, normed_half, preferred_element_type=jnp.float32
    ).astype(jnp.bfloat16)
    received = lax.all_to_all(send_rows, "req", 0, 0, tiled=True)
    partner_rows = lax.ppermute(received, "tc", [(0, 1), (1, 0)])
    weight_blocks = w_gate_up[0].reshape(column_groups, 2, slice_width, 2, units_dev)
    own_weights = lax.dynamic_index_in_dim(weight_blocks, tc, axis=1, keepdims=False).reshape(
        model_width // 2, 2, units_dev
    )
    partner_weights = lax.dynamic_index_in_dim(
        weight_blocks, 1 - tc, axis=1, keepdims=False
    ).reshape(model_width // 2, 2, units_dev)
    gate_up = jnp.einsum(
        "scw,wgu->scgu", received, own_weights, preferred_element_type=jnp.float32
    ) + jnp.einsum(
        "scw,wgu->scgu", partner_rows, partner_weights, preferred_element_type=jnp.float32
    )
    activated = (jax.nn.silu(gate_up[..., 0, :]) * gate_up[..., 1, :]).astype(jnp.bfloat16)
    down = (
        w_down[0]
        .reshape(units_dev, 2, 2, 2, slice_width)
        .transpose(0, 3, 2, 1, 4)
        .reshape(units_dev, model_width)
    )
    partial = jnp.einsum(
        "scu,uw->scw", activated, down, preferred_element_type=jnp.float32
    ).astype(jnp.bfloat16)
    swap = [(0, 1), (1, 0)]
    half = model_width // 2
    kept = lax.dynamic_slice_in_dim(partial, tc * half, half, 2)
    given = lax.dynamic_slice_in_dim(partial, (1 - tc) * half, half, 2)
    pair_sum = kept.astype(jnp.float32) + lax.ppermute(given, "tc", swap).astype(jnp.float32)
    quarter = half // 2
    kept = lax.dynamic_slice_in_dim(pair_sum, tl * quarter, quarter, 2)
    given = lax.dynamic_slice_in_dim(pair_sum, (1 - tl) * quarter, quarter, 2).astype(jnp.bfloat16)
    quad_sum = (kept + lax.ppermute(given, "tl", swap).astype(jnp.float32)).astype(jnp.bfloat16)
    back = (
        quad_sum.reshape(req_count, capacity, 2, slice_width)
        .transpose(0, 2, 1, 3)
        .reshape(req_count * 2, capacity, slice_width)
    )
    returned = lax.all_to_all(back, ("req", "th"), 0, 0, tiled=True)
    combine = weight_of[:, :, None] * (slot_of[:, :, None] == cap_ids[None, None, :])
    mixture = jnp.dot(
        combine.reshape(tok_rows, EXPERTS * capacity),
        returned.reshape(EXPERTS * capacity, slice_width).astype(jnp.float32),
        precision=lax.Precision.HIGHEST,
        preferred_element_type=jnp.float32,
    )
    output = (residual_share + mixture).astype(jnp.bfloat16)
    picked_rows = (jnp.arange(req_local, dtype=jnp.int32)[:, None] * draft_len + accepted).reshape(
        -1
    )
    accepted_kv = jnp.stack(
        [keys_new.reshape(tok_rows, feat_dev)[picked_rows], values_new[picked_rows]]
    )
    return (output, accepted_kv)


def solution(mesh):
    req_count = mesh.shape["req"]
    devices = mesh.devices.reshape(req_count, 2, 2, mesh.shape["tp"] // 4)
    split_mesh = Mesh(devices, ("req",) + TP)
    return jax.shard_map(
        local,
        mesh=split_mesh,
        in_specs=(
            P("req", None),
            P(None, "req", None, TP),
            P("req", None),
            P("req"),
            P("req", None),
            P("req", None),
            P(),
            P(None, None, TP),
            P(None, TP),
            P(TP, None),
            P(),
            P("req", None),
            P("req", None),
            P("req", None, None, TP),
            P("req", TP, None),
        ),
        out_specs=(P("req", TP), P(None, "req", TP)),
        check_vma=False,
    )
```

profile of v0, /device:TPU:32, one launch (start us, length us, event | category | flops | bytes accessed | tf_op | source)
XLA Modules:
  0.0 287.1 jit_solution(17295644223071763492)
XLA Ops:
  2.8 2.7 fusion.41
  8.4 4.1 %fusion.93 = (bf16[1,32,128,256]{3,2,1,0:T(8,128)(2,1)}, bf16[1,32,128,256]{3,2,1,0:T(8,128)(2,1)S(1)}) fusion(bf16[2,32,128,256]{3,2,1,0:T(8,128)(2,1)} %param.16), kind=kLoop, calls=%fused_computation.186 | loop fusion | bytes 8388608 | tf_op jit(solution)/shard_map/slice | solution.py:102
  14.6 2.0 collective-permute-done.1
  16.6 3.5 %collective-permute-start.2 = (f32[2,256]{1,0:T(2,128)S(1)}, f32[2,256]{1,0:T(2,128)S(1)}, u32[]{:S(2)}, u32[]{:S(2)}) collective-permute-start(f32[2,256]{1,0:T(2,128)S(1)} %fusion.128), channel_id=1, source_target_pairs={{0,4},{4,0},{1,5},{5,1},{2,6},{6,2},{3,7},{7,3},{8,12},{12,8},{9,1... | collective-permute-start | bytes 6152 | tf_op jit(solution)/shard_map/ppermute | solution.py:93
  30.2 1.8 fusion.58
  32.0 3.0 %reshape.402 = f32[256,4,2,256]{3,2,1,0:T(2,128)S(1)} reshape(f32[256,2048]{1,0:T(8,128)} %fusion.58) | data formatting | bytes 4194304 | tf_op jit(solution)/shard_map/reshape | solution.py:151
  35.1 1.8 constant_dynamic-slice_fusion.8
  37.5 2.6 collective-permute-done.3
  44.0 12.4 %collective-permute-done.4 = f32[256,2,256]{2,0,1:T(8,128)S(1)} collective-permute-done((f32[256,2,256]{2,0,1:T(8,128)S(1)}, f32[256,2,256]{2,0,1:T(8,128)S(1)}, u32[]{:S(2)}, u32[]{:S(2)}) %collective-permute-start.4) | collective-permute-done | bytes 524320 | tf_op jit(solution)/shard_map/ppermute | solution.py:157
  57.2 3.2 %collective-permute-start.5 = (f32[256,256]{1,0:T(8,128)}, f32[256,256]{1,0:T(8,128)}, u32[]{:S(2)}, u32[]{:S(2)}) collective-permute-start(f32[256,256]{1,0:T(8,128)} %dynamic-slice_bitcast_fusion), channel_id=1, source_target_pairs={{0,4},{4,0},{1,5},{5,1},{2,6},{6,2},{3,7},{7,3},{8,12},{12,8},{9,1... | collective-permute-start | bytes 786440 | tf_op jit(solution)/shard_map/ppermute | solution.py:160
  60.4 2.1 reshape.397
  62.6 3.5 %fusion.92 = (f32[256,4,256]{2,1,0:T(4,128)S(1)}, f32[256,4,1,256]{3,2,1,0:T(1,128)}) fusion(f32[256,4,2,256]{3,2,1,0:T(2,128)S(1)} %reshape.397, s32[]{:T(128)S(6)} %select_n.110), kind=kLoop, calls=%fused_computation.185 | loop fusion | bytes 3145732 | tf_op jit(solution)/shard_map/jit(dynamic_index_in_dim)/dynamic_slice | solution.py:175
  67.5 3.3 %collective-permute-start.6 = (f32[256,256]{1,0:T(8,128)S(1)}, f32[256,256]{1,0:T(8,128)S(1)}, u32[]{:S(2)}, u32[]{:S(2)}) collective-permute-start(f32[256,256]{1,0:T(8,128)S(1)} %bitcast_add_fusion.3), channel_id=1, source_target_pairs={{0,4},{4,0},{1,5},{5,1},{2,6},{6,2},{3,7},{7,3},{8,12},{12,8},{9,1... | collective-permute-start | bytes 786440 | tf_op jit(solution)/shard_map/ppermute | solution.py:163
  71.9 3.9 %collective-permute-done.6 = f32[256,256]{1,0:T(8,128)S(1)} collective-permute-done((f32[256,256]{1,0:T(8,128)S(1)}, f32[256,256]{1,0:T(8,128)S(1)}, u32[]{:S(2)}, u32[]{:S(2)}) %collective-permute-start.6) | collective-permute-done | bytes 262176 | tf_op jit(solution)/shard_map/ppermute | solution.py:163
  77.6 1.9 collective-permute-start.7
  80.6 9.3 %collective-permute-done.7 = f32[256,2,256]{2,1,0:T(2,128)} collective-permute-done((f32[256,2,256]{2,1,0:T(2,128)}, f32[256,2,256]{2,1,0:T(2,128)}, u32[]{:S(2)}, u32[]{:S(2)}) %collective-permute-start.7) | collective-permute-done | bytes 524320 | tf_op jit(solution)/shard_map/ppermute | solution.py:169
  95.5 1.9 select_n.129
  97.4 2.6 convolution_convert_fusion.1
  100.0 73.7 %all_to_all.10 = bf16[32,40,1024]{2,1,0:T(8,128)(2,1)} all-to-all(bf16[32,40,1024]{2,1,0:T(8,128)(2,1)S(1)} %convolution_convert_fusion.1), channel_id=1, replica_groups=mesh['req'=32,'th'=2,'tl'=2,'tc'=2] {'req'}, dimensions={0} | all-to-all | bytes 5242880 | tf_op jit(solution)/shard_map/all_to_all | solution.py:209
  173.8 1.8 reshape_squeeze.31
  177.6 3.0 %constant_dynamic-slice_fusion.1 = (bf16[4,1,256,2,256]{4,3,2,1,0:T(2,128)(2,1)S(1)}, bf16[4,1,256,2,256]{4,3,2,1,0:T(2,128)(2,1)S(1)}) fusion(bf16[4,2,256,2,256]{4,3,2,1,0:T(2,128)(2,1)} %bitcast.163, s32[]{:T(128)S(6)} %select_n.117, s32[]{:T(128)S(6)} %select_n.110), kind=kLoop, calls=%fused_computation.151 | loop fusion | bytes 4194312 | tf_op jit(solution)/shard_map/jit(dynamic_index_in_dim)/dynamic_slice | solution.py:215
  181.9 3.4 %fusion.6 = f32[32,40,2,256]{3,1,2,0:T(8,128)S(1)} fusion(bf16[1024,2,256,1]{2,0,1,3:T(8,128)(2,1)S(1)} %bitcast.169, bf16[32,40,1024]{2,1,0:T(8,128)(2,1)} %all_to_all.10), kind=kOutput, calls=%fused_computation.16 | convolution fusion | flops 1342177280 | bytes 6291456 | tf_op jit(solution)/shard_map/scw,wgu->scgu/dot_general | solution.py:218
  185.3 3.4 %fusion.12 = f32[32,40,2,256]{3,1,2,0:T(8,128)S(1)} fusion(f32[32,40,2,256]{3,1,2,0:T(8,128)S(1)} %fusion.6, bf16[1024,2,256,1]{2,0,1,3:T(8,128)(2,1)S(1)} %bitcast.168, bf16[32,40,1024]{2,1,0:T(8,128)(2,1)} %collective-permute-done.9), kind=kOutput, calls=%fused_computation.28 | convolution fusion | flops 1342832640 | bytes 8912896 | tf_op jit(solution)/shard_map/scw,wgu->scgu/dot_general | solution.py:220
  190.6 2.0 copy-done.3
  193.1 4.7 %collective-permute-done.10 = bf16[32,40,1024]{2,1,0:T(8,128)(2,1)} collective-permute-done((bf16[32,40,1024]{2,1,0:T(8,128)(2,1)S(1)}, bf16[32,40,1024]{2,1,0:T(8,128)(2,1)}, u32[]{:S(2)}, u32[]{:S(2)}) %collective-permute-start.10) | collective-permute-done | bytes 2621472 | tf_op jit(solution)/shard_map/ppermute | solution.py:237
  197.8 3.7 %convert_add_fusion = f32[32,40,1024]{2,1,0:T(8,128)S(1)} fusion(bf16[32,40,1024]{2,1,0:T(8,128)(2,1)} %collective-permute-done.10, bf16[32,40,2048]{2,1,0:T(8,128)(2,1)} %copy-done.3, s32[]{:T(128)S(6)} %select_n.130), kind=kLoop, calls=%fused_computation.6 | loop fusion | flops 3932160 | bytes 10485764 | tf_op jit(solution)/shard_map/add | solution.py:237
  201.5 2.3 copy-done.2
  205.4 29.7 %collective-permute-done.11 = bf16[32,40,512]{2,1,0:T(8,128)(2,1)S(1)} collective-permute-done((bf16[32,40,512]{2,1,0:T(8,128)(2,1)S(1)}, bf16[32,40,512]{2,1,0:T(8,128)(2,1)S(1)}, u32[]{:S(2)}, u32[]{:S(2)}) %collective-permute-start.11) | collective-permute-done | bytes 1310752 | tf_op jit(solution)/shard_map/ppermute | solution.py:241
  235.1 2.2 add_convert_fusion
  238.6 8.4 %all-to-all-start.1 = ((bf16[64,40,256]{2,1,0:T(8,128)(2,1)}), bf16[64,40,256]{2,1,0:T(8,128)(2,1)}, u32[]{:S(2)}, u32[]{:S(2)}) async-start(bf16[64,40,256]{2,1,0:T(8,128)(2,1)} %bitcast.49), calls=%async_computation.1 | async-start | bytes 2621440 | tf_op jit(solution)/shard_map/all_to_all | solution.py:247
  249.3 33.1 %all-to-all-done.1 = bf16[64,40,256]{2,1,0:T(8,128)(2,1)} async-done(((bf16[64,40,256]{2,1,0:T(8,128)(2,1)}), bf16[64,40,256]{2,1,0:T(8,128)(2,1)}, u32[]{:S(2)}, u32[]{:S(2)}) %all-to-all-start.1) | async-done | bytes 1310752 | tf_op jit(solution)/shard_map/all_to_all | solution.py:247
  282.4 4.5 %fusion.31 = bf16[256,256]{1,0:T(8,128)(2,1)} fusion(bf16[64,40,256]{2,1,0:T(8,128)(2,1)} %all-to-all-done.1, f32[256,64]{0,1:T(8,128)S(1)} %copy-done.11, f32[256,64]{0,1:T(8,128)S(1)} %fusion.56, f32[256,4,256]{2,0,1:T(8,128)} %get-tuple-element.9, s32[]{:T(128)S(6)} %select_n.127), kind=kOutput, calls=%fused_computation.41 | convolution fusion | flops 2014707712 | bytes 1835012 | tf_op jit(solution)/shard_map/dot_general | solution.py:249
  (160 shorter events, 44.2 us)
Async XLA Ops:
  0.6 2.2 copy-start
  2.8 3.0 %copy-start.16 = (s32[4,8]{1,0:T(4,128)S(1)}, s32[4,8]{1,0:T(4,128)}, u32[]{:S(2)}) copy-start(s32[4,8]{1,0:T(4,128)} %param.17) | copy-start | bytes 388
  2.8 3.3 %copy-start.19 = (s32[4,64]{1,0:T(4,128)S(1)}, s32[4,64]{1,0:T(4,128)}, u32[]{:S(2)}) copy-start(s32[4,64]{1,0:T(4,128)} %param.19) | copy-start | bytes 3076
  5.5 2.6 copy-start.15
  5.6 7.2 %collective-permute-start = (f32[2,256]{1,0:T(2,128)S(1)}, f32[2,256]{1,0:T(2,128)S(1)}, u32[]{:S(2)}, u32[]{:S(2)}) collective-permute-start(f32[2,256]{1,0:T(2,128)S(1)} %pad_maximum_fusion.5), channel_id=1, source_target_pairs={{0,1},{1,0},{2,3},{3,2},{4,5},{5,4},{6,7},{7,6},{8,9},{9,8},{10,11... | collective-permute-start | bytes 6152 | tf_op jit(solution)/shard_map/ppermute | solution.py:91
  8.3 11.7 %copy-start.17 = (f32[2,256]{1,0:T(2,128)S(1)}, f32[2,256]{1,0:T(2,128)}, u32[]{:S(2)}) copy-start(f32[2,256]{1,0:T(2,128)} %param.23) | copy-start | bytes 6148
  12.9 3.7 %collective-permute-start.1 = (f32[2,256]{1,0:T(2,128)S(1)}, f32[2,256]{1,0:T(2,128)S(1)}, u32[]{:S(2)}, u32[]{:S(2)}) collective-permute-start(f32[2,256]{1,0:T(2,128)S(1)} %fusion.91), channel_id=1, source_target_pairs={{0,2},{2,0},{1,3},{3,1},{4,6},{6,4},{5,7},{7,5},{8,10},{10,8},{9,1... | collective-permute-start | bytes 6152 | tf_op jit(solution)/shard_map/ppermute | solution.py:92
  16.6 5.4 %collective-permute-start.2 = (f32[2,256]{1,0:T(2,128)S(1)}, f32[2,256]{1,0:T(2,128)S(1)}, u32[]{:S(2)}, u32[]{:S(2)}) collective-permute-start(f32[2,256]{1,0:T(2,128)S(1)} %fusion.128), channel_id=1, source_target_pairs={{0,4},{4,0},{1,5},{5,1},{2,6},{6,2},{3,7},{7,3},{8,12},{12,8},{9,1... | collective-permute-start | bytes 6152 | tf_op jit(solution)/shard_map/ppermute | solution.py:93
  26.0 1.6 copy-start.8
  37.2 3.0 %collective-permute-start.3 = (f32[256,4,256]{2,1,0:T(4,128)S(1)}, f32[256,4,256]{2,1,0:T(4,128)S(1)}, u32[]{:S(2)}, u32[]{:S(2)}) collective-permute-start(f32[256,4,256]{2,1,0:T(4,128)S(1)} %bitcast.167), channel_id=1, source_target_pairs={{0,1},{1,0},{2,3},{3,2},{4,5},{5,4},{6,7},{7,6},{8,9},{9,8},{10,11... | collective-permute-start | bytes 3145736 | tf_op jit(solution)/shard_map/ppermute | solution.py:154
  41.3 19.1 %copy-start.4 = (bf16[256,2048]{1,0:T(8,128)(2,1)S(1)}, bf16[256,2048]{1,0:T(8,128)(2,1)}, u32[]{:S(2)}) copy-start(bf16[256,2048]{1,0:T(8,128)(2,1)} %param.15) | copy-start | bytes 3145732
  42.3 14.1 %collective-permute-start.4 = (f32[256,2,256]{2,0,1:T(8,128)S(1)}, f32[256,2,256]{2,0,1:T(8,128)S(1)}, u32[]{:S(2)}, u32[]{:S(2)}) collective-permute-start(f32[256,2,256]{2,0,1:T(8,128)S(1)} %bitcast.177), channel_id=1, source_target_pairs={{0,2},{2,0},{1,3},{3,1},{4,6},{6,4},{5,7},{7,5},{8,10},{10,8},{9,1... | collective-permute-start | bytes 1572872 | tf_op jit(solution)/shard_map/ppermute | solution.py:157
  56.4 4.0 %copy-start.6 = (f32[256,2,256]{2,0,1:T(8,128)}, f32[256,2,256]{2,0,1:T(8,128)S(1)}, u32[]{:S(2)}) copy-start(f32[256,2,256]{2,0,1:T(8,128)S(1)} %bitcast_add_fusion.2) | copy-start | bytes 1572868
  57.2 9.3 %collective-permute-start.5 = (f32[256,256]{1,0:T(8,128)}, f32[256,256]{1,0:T(8,128)}, u32[]{:S(2)}, u32[]{:S(2)}) collective-permute-start(f32[256,256]{1,0:T(8,128)} %dynamic-slice_bitcast_fusion), channel_id=1, source_target_pairs={{0,4},{4,0},{1,5},{5,1},{2,6},{6,2},{3,7},{7,3},{8,12},{12,8},{9,1... | collective-permute-start | bytes 786440 | tf_op jit(solution)/shard_map/ppermute | solution.py:160
  62.5 8.3 %copy-start.12 = (f32[256,8]{0,1:T(8,128)S(1)}, f32[256,8]{0,1:T(8,128)}, u32[]{:S(2)}) copy-start(f32[256,8]{0,1:T(8,128)} %param.27) | copy-start | bytes 24580
  62.5 8.3 %copy-start.13 = (s32[256,8]{0,1:T(8,128)S(1)}, s32[256,8]{0,1:T(8,128)}, u32[]{:S(2)}) copy-start(s32[256,8]{0,1:T(8,128)} %param.26) | copy-start | bytes 24580
  62.5 4.0 %copy-start.7 = (f32[256,2,256]{2,0,1:T(8,128)S(1)}, f32[256,2,256]{2,0,1:T(8,128)}, u32[]{:S(2)}) copy-start(f32[256,2,256]{2,0,1:T(8,128)} %copy-done.6) | copy-start | bytes 1572868
  62.5 17.0 %copy-start.14 = (f32[2048]{0:T(1024)S(1)}, f32[2048]{0:T(1024)}, u32[]{:S(2)}) copy-start(f32[2048]{0:T(1024)} %param.25) | copy-start | bytes 24580
  67.5 8.3 %collective-permute-start.6 = (f32[256,256]{1,0:T(8,128)S(1)}, f32[256,256]{1,0:T(8,128)S(1)}, u32[]{:S(2)}, u32[]{:S(2)}) collective-permute-start(f32[256,256]{1,0:T(8,128)S(1)} %bitcast_add_fusion.3), channel_id=1, source_target_pairs={{0,4},{4,0},{1,5},{5,1},{2,6},{6,2},{3,7},{7,3},{8,12},{12,8},{9,1... | collective-permute-start | bytes 786440 | tf_op jit(solution)/shard_map/ppermute | solution.py:163
  77.6 12.3 %collective-permute-start.7 = (f32[256,2,256]{2,1,0:T(2,128)}, f32[256,2,256]{2,1,0:T(2,128)}, u32[]{:S(2)}, u32[]{:S(2)}) collective-permute-start(f32[256,2,256]{2,1,0:T(2,128)} %maximum_select_fusion.1), channel_id=1, source_target_pairs={{0,2},{2,0},{1,3},{3,1},{4,6},{6,4},{5,7},{7,5},{8,10},{10,8},{9,1... | collective-permute-start | bytes 1572872 | tf_op jit(solution)/shard_map/ppermute | solution.py:169
  80.6 12.4 %copy-start.5 = (f32[256,4,1,256]{3,2,1,0:T(1,128)S(1)}, f32[256,4,1,256]{3,2,1,0:T(1,128)}, u32[]{:S(2)}) copy-start(f32[256,4,1,256]{3,2,1,0:T(1,128)} %get-tuple-element.11) | copy-start | bytes 3145732
  94.3 3.1 %collective-permute-start.8 = (f32[256]{0:T(256)S(1)}, f32[256]{0:T(256)S(1)}, u32[]{:S(2)}, u32[]{:S(2)}) collective-permute-start(f32[256]{0:T(256)S(1)} %get-tuple-element.8), channel_id=1, source_target_pairs={{0,1},{1,0},{2,3},{3,2},{4,5},{5,4},{6,7},{7,6},{8,9},{9,8},{10,11... | collective-permute-start | bytes 3080 | tf_op jit(solution)/shard_map/ppermute | solution.py:177
  173.7 11.6 %collective-permute-start.9 = (bf16[32,40,1024]{2,1,0:T(8,128)(2,1)}, bf16[32,40,1024]{2,1,0:T(8,128)(2,1)}, u32[]{:S(2)}, u32[]{:S(2)}) collective-permute-start(bf16[32,40,1024]{2,1,0:T(8,128)(2,1)} %all_to_all.10), channel_id=1, source_target_pairs={{0,1},{1,0},{2,3},{3,2},{4,5},{5,4},{6,7},{7,6},{8,9},{9,8},{10,11... | collective-permute-start | bytes 7864328 | tf_op jit(solution)/shard_map/ppermute | solution.py:210
  181.9 3.4 %copy-start.10 = (bf16[4,1,256,2,256]{4,2,0,3,1:T(8,128)(2,1)S(1)}, bf16[4,1,256,2,256]{4,2,0,3,1:T(8,128)(2,1)}, u32[]{:S(2)}) copy-start(bf16[4,1,256,2,256]{4,2,0,3,1:T(8,128)(2,1)} %copy.151) | copy-start | bytes 3145732
  190.3 2.3 copy-start.3
  192.6 5.2 %collective-permute-start.10 = (bf16[32,40,1024]{2,1,0:T(8,128)(2,1)S(1)}, bf16[32,40,1024]{2,1,0:T(8,128)(2,1)}, u32[]{:S(2)}, u32[]{:S(2)}) collective-permute-start(bf16[32,40,1024]{2,1,0:T(8,128)(2,1)S(1)} %constant_dynamic-slice_fusion), channel_id=1, source_target_pairs={{0,1},{1,0},{2,3},{3,2},{4,5},{5,4},{6,7},{7,6},{8,9},{9,8},{10,11... | collective-permute-start | bytes 7864328 | tf_op jit(solution)/shard_map/ppermute | solution.py:237
  201.5 2.3 copy-start.2
  204.0 31.1 %collective-permute-start.11 = (bf16[32,40,512]{2,1,0:T(8,128)(2,1)S(1)}, bf16[32,40,512]{2,1,0:T(8,128)(2,1)S(1)}, u32[]{:S(2)}, u32[]{:S(2)}) collective-permute-start(bf16[32,40,512]{2,1,0:T(8,128)(2,1)S(1)} %dynamic-slice_convert_fusion), channel_id=1, source_target_pairs={{0,2},{2,0},{1,3},{3,1},{4,6},{6,4},{5,7},{7,5},{8,10},{10,8},{9,1... | collective-permute-start | bytes 3932168 | tf_op jit(solution)/shard_map/ppermute | solution.py:241
  237.4 9.7 %copy-start.18 = (s32[4,8]{1,0:T(4,128)S(1)}, s32[4,8]{1,0:T(4,128)}, u32[]{:S(2)}) copy-start(s32[4,8]{1,0:T(4,128)} %param.20) | copy-start | bytes 388
  237.4 45.0 %copy-start.11 = (f32[256,64]{0,1:T(8,128)S(1)}, f32[256,64]{0,1:T(8,128)}, u32[]{:S(2)}) copy-start(f32[256,64]{0,1:T(8,128)} %get-tuple-element.4) | copy-start | bytes 196612
  238.6 43.8 %all-to-all-start.1 = ((bf16[64,40,256]{2,1,0:T(8,128)(2,1)}), bf16[64,40,256]{2,1,0:T(8,128)(2,1)}, u32[]{:S(2)}, u32[]{:S(2)}) async-start(bf16[64,40,256]{2,1,0:T(8,128)(2,1)} %bitcast.49), calls=%async_computation.1 | async-start | bytes 2621440 | tf_op jit(solution)/shard_map/all_to_all | solution.py:247
  282.4 4.5 %copy-start.1 = (bf16[2048,3,256]{2,0,1:T(8,128)(2,1)S(1)}, bf16[2048,3,256]{2,0,1:T(8,128)(2,1)}, u32[]{:S(2)}) copy-start(bf16[2048,3,256]{2,0,1:T(8,128)(2,1)} %param.22) | copy-start | bytes 9437188
  (1 other events, 1.6 us)
where the time goes:
time: 292 us; the launch traced here: 287 us
  waiting for transfers between devices  99.8 us (34%)
  blocking collectives  73.7 us (25%)
  local copies, waits for them, and re-layouts  39.1 us (13%)
  matrix products  26.9 us (9%)
  starting transfers between devices  26.1 us (9%)
  other arithmetic  19.8 us (7%)
    all_to_all x1, blocking collectives, local(): received = lax.all_to_all(send_rows, 'req', 0, 0, tiled=True)  73.7 us
    all_to_all x1, waiting for transfers between devices, local(): returned = lax.all_to_all(back, ('req', 'th'), 0, 0, tiled=True)  33.1 us
    ppermute x1, waiting for transfers between devices, local(): lax.ppermute(given, 'tl', swap).astype(jnp.float32)  29.7 us
    ppermute x1, waiting for transfers between devices, local(): lax.ppermute(lax.dynamic_index_in_dim(pair_blocks, 1 - tl, axis=2, keepdi...  12.4 us
    ppermute x1, waiting for transfers between devices, local(): row_other = lax.ppermute(row_sum, 'tl', swap)  9.26 us
    unnamed x48, local copies, waits for them, and re-layouts  8.47 us
    all_to_all x1, starting transfers between devices, local(): returned = lax.all_to_all(back, ('req', 'th'), 0, 0, tiled=True)  8.4 us
  transfers between devices with their start and end apart: 13, of which 10 were waited for; matrix products, arithmetic and copies ran while one was open for 11% of the time, Pallas kernels for 0%

commit v1 on v0

--- a/solution.py
+++ b/solution.py
@@ -151,22 +151,26 @@
     attn_blocks = attn_term.reshape(tok_rows, column_groups, 2, slice_width)
     kept = lax.dynamic_index_in_dim(attn_blocks, tc, axis=2, keepdims=False)
     given = lax.dynamic_index_in_dim(attn_blocks, 1 - tc, axis=2, keepdims=False)
-    chip_sum = kept + lax.ppermute(given, "tc", swap)
+    chip_sum = kept + lax.ppermute(given.astype(jnp.bfloat16), "tc", swap).astype(jnp.float32)
     hidden_blocks = hidden.astype(jnp.float32).reshape(tok_rows, column_groups, 2, slice_width)
     pair_blocks = chip_sum.reshape(tok_rows, column_groups // 2, 2, slice_width)
     row_sum = lax.dynamic_index_in_dim(pair_blocks, tl, axis=2, keepdims=False) + lax.ppermute(
-        lax.dynamic_index_in_dim(pair_blocks, 1 - tl, axis=2, keepdims=False), "tl", swap
-    )
+        lax.dynamic_index_in_dim(pair_blocks, 1 - tl, axis=2, keepdims=False).astype(jnp.bfloat16),
+        "tl",
+        swap,
+    ).astype(jnp.float32)
     block_sum = lax.dynamic_index_in_dim(row_sum, th, axis=1, keepdims=False) + lax.ppermute(
-        lax.dynamic_index_in_dim(row_sum, 1 - th, axis=1, keepdims=False), "th", swap
-    )
-    block_other = lax.ppermute(block_sum, "th", swap)
+        lax.dynamic_index_in_dim(row_sum, 1 - th, axis=1, keepdims=False).astype(jnp.bfloat16),
+        "th",
+        swap,
+    ).astype(jnp.float32)
+    block_other = lax.ppermute(block_sum.astype(jnp.bfloat16), "th", swap).astype(jnp.float32)
     row_sum = jnp.where(
         th == 0,
         jnp.stack([block_sum, block_other], axis=1),
         jnp.stack([block_other, block_sum], axis=1),
     )
-    row_other = lax.ppermute(row_sum, "tl", swap)
+    row_other = lax.ppermute(row_sum.astype(jnp.bfloat16), "tl", swap).astype(jnp.float32)
     full_sum = jnp.where(
         tl == 0,
         jnp.stack([row_sum, row_other], axis=2),

time: 292 us -> 273 us (0.935)
  waiting for transfers between devices: 99.8 us -> 84 us
    ppermute x1, waiting for transfers between devices: 12.4 us -> 3.93 us  [local(): lax.ppermute(lax.dynamic_index_in_dim(pair_blocks, 1 - tl, axis=2, keepdi...]
    ppermute x3, waiting for transfers between devices: 15.8 us -> 8.98 us  [the longest x1 4.92 us: local(): lax.ppermute(row_sum.astype(jnp.bfloat16), 'tl', swap).astype(jnp.float32)]
    unnamed x48 -> x46, local copies, waits for them, and re-layouts: 8.47 us -> 9.18 us
  transfers between devices with their start and end apart: 13 -> 13, of which waited for: 10 -> 9; matrix products, arithmetic and copies ran while one was open for 11% -> 12% of each run, Pallas kernels for 0% -> 0%
where the time goes in v1:
time: 273 us; the launch traced here: 268 us
  waiting for transfers between devices  84 us (31%)
  blocking collectives  73.7 us (27%)
  local copies, waits for them, and re-layouts  37.7 us (14%)
  matrix products  26.9 us (10%)
  starting transfers between devices  25.9 us (9%)
  other arithmetic  17.8 us (7%)
    all_to_all x1, blocking collectives, local(): received = lax.all_to_all(send_rows, 'req', 0, 0, tiled=True)  73.7 us
    all_to_all x1, waiting for transfers between devices, local(): returned = lax.all_to_all(back, ('req', 'th'), 0, 0, tiled=True)  33.1 us
    ppermute x1, waiting for transfers between devices, local(): lax.ppermute(given, 'tl', swap).astype(jnp.float32)  29.7 us
    unnamed x46, local copies, waits for them, and re-layouts  9.18 us
    all_to_all x1, starting transfers between devices, local(): returned = lax.all_to_all(back, ('req', 'th'), 0, 0, tiled=True)  8.69 us
  transfers between devices with their start and end apart: 13, of which 9 were waited for; matrix products, arithmetic and copies ran while one was open for 12% of the time, Pallas kernels for 0%

profile of v1, /device:TPU:32, one launch (start us, length us, event | category | flops | bytes accessed | tf_op | source)
XLA Modules:
  0.0 267.6 jit_solution(14881594535555736158)
XLA Ops:
  0.6 1.7 multiply_reduce_fusion
  2.8 2.7 %fusion.41 = f32[256,3,256]{0,2,1:T(8,128)S(1)} fusion(bf16[2048,3,256]{2,0,1:T(8,128)(2,1)S(1)} %copy-done, f32[2048]{0:T(1024)} %param.21, f32[256]{0:T(256)S(1)} %add_rsqrt_fusion.1, bf16[256,2048]{1,0:T(8,128)(2,1)} %param.15), kind=kOutput, calls=%fused_computation.58 | convolution fusion | flops 807403520 | bytes 4989952 | tf_op jit(solution)/shard_map/tw,wgf->tgf/dot_general | solution.py:81
  8.4 4.1 %fusion.100 = (bf16[1,32,128,256]{3,2,1,0:T(8,128)(2,1)}, bf16[1,32,128,256]{3,2,1,0:T(8,128)(2,1)S(1)}) fusion(bf16[2,32,128,256]{3,2,1,0:T(8,128)(2,1)} %param.16), kind=kLoop, calls=%fused_computation.192 | loop fusion | bytes 8388608 | tf_op jit(solution)/shard_map/slice | solution.py:102
  12.9 1.7 collective-permute-start.1
  14.6 2.0 collective-permute-done.1
  16.6 3.5 %collective-permute-start.2 = (f32[2,256]{1,0:T(2,128)S(1)}, f32[2,256]{1,0:T(2,128)S(1)}, u32[]{:S(2)}, u32[]{:S(2)}) collective-permute-start(f32[2,256]{1,0:T(2,128)S(1)} %fusion.135), channel_id=1, source_target_pairs={{0,4},{4,0},{1,5},{5,1},{2,6},{6,2},{3,7},{7,3},{8,12},{12,8},{9,1... | collective-permute-start | bytes 6152 | tf_op jit(solution)/shard_map/ppermute | solution.py:93
  30.2 1.8 fusion.62
  32.0 3.0 %reshape.405 = f32[256,4,2,256]{3,2,1,0:T(2,128)S(1)} reshape(f32[256,2048]{1,0:T(8,128)} %fusion.62) | data formatting | bytes 4194304 | tf_op jit(solution)/shard_map/reshape | solution.py:151
  41.3 1.8 collective-permute-start.4
  43.9 2.1 reshape.400
  46.2 3.9 %collective-permute-done.4 = bf16[256,2,256]{2,0,1:T(8,128)(2,1)} collective-permute-done((bf16[256,2,256]{2,0,1:T(8,128)(2,1)}, bf16[256,2,256]{2,0,1:T(8,128)(2,1)}, u32[]{:S(2)}, u32[]{:S(2)}) %collective-permute-start.4) | collective-permute-done | bytes 262176 | tf_op jit(solution)/shard_map/ppermute | solution.py:157
  51.4 3.3 %collective-permute-start.5 = (bf16[256,256]{1,0:T(8,128)(2,1)S(1)}, bf16[256,256]{1,0:T(8,128)(2,1)S(1)}, u32[]{:S(2)}, u32[]{:S(2)}) collective-permute-start(bf16[256,256]{1,0:T(8,128)(2,1)S(1)} %fusion.60), channel_id=1, source_target_pairs={{0,4},{4,0},{1,5},{5,1},{2,6},{6,2},{3,7},{7,3},{8,12},{12,8},{9,1... | collective-permute-start | bytes 393224 | tf_op jit(solution)/shard_map/ppermute | solution.py:162
  54.7 3.5 %fusion.99 = (f32[256,4,256]{2,1,0:T(4,128)S(1)}, f32[256,4,1,256]{3,2,1,0:T(1,128)S(1)}) fusion(f32[256,4,2,256]{3,2,1,0:T(2,128)S(1)} %reshape.400, s32[]{:T(128)S(6)} %select_n.110), kind=kLoop, calls=%fused_computation.191 | loop fusion | bytes 3145732 | tf_op jit(solution)/shard_map/jit(dynamic_index_in_dim)/dynamic_slice | solution.py:179
  58.2 3.1 %collective-permute-start.6 = (bf16[256,256]{1,0:T(8,128)(2,1)S(1)}, bf16[256,256]{1,0:T(8,128)(2,1)S(1)}, u32[]{:S(2)}, u32[]{:S(2)}) collective-permute-start(bf16[256,256]{1,0:T(8,128)(2,1)S(1)} %get-tuple-element.21), channel_id=1, source_target_pairs={{0,4},{4,0},{1,5},{5,1},{2,6},{6,2},{3,7},{7,3},{8,12},{12,8},{9,1... | collective-permute-start | bytes 393224 | tf_op jit(solution)/shard_map/ppermute | solution.py:167
  61.3 3.4 %collective-permute-done.6 = bf16[256,256]{1,0:T(8,128)(2,1)S(1)} collective-permute-done((bf16[256,256]{1,0:T(8,128)(2,1)S(1)}, bf16[256,256]{1,0:T(8,128)(2,1)S(1)}, u32[]{:S(2)}, u32[]{:S(2)}) %collective-permute-start.6) | collective-permute-done | bytes 131104 | tf_op jit(solution)/shard_map/ppermute | solution.py:167
  66.3 4.9 %collective-permute-done.7 = bf16[256,2,256]{2,0,1:T(8,128)(2,1)S(1)} collective-permute-done((bf16[256,2,256]{2,0,1:T(8,128)(2,1)S(1)}, bf16[256,2,256]{2,0,1:T(8,128)(2,1)S(1)}, u32[]{:S(2)}, u32[]{:S(2)}) %collective-permute-start.7) | collective-permute-done | bytes 262176 | tf_op jit(solution)/shard_map/ppermute | solution.py:173
  74.8 1.9 select_n.129
  77.4 2.6 convolution_convert_fusion.1
  80.0 73.7 %all_to_all.10 = bf16[32,40,1024]{2,1,0:T(8,128)(2,1)} all-to-all(bf16[32,40,1024]{2,1,0:T(8,128)(2,1)S(1)} %convolution_convert_fusion.1), channel_id=1, replica_groups=mesh['req'=32,'th'=2,'tl'=2,'tc'=2] {'req'}, dimensions={0} | all-to-all | bytes 5242880 | tf_op jit(solution)/shard_map/all_to_all | solution.py:213
  154.0 1.8 reshape_squeeze.31
  157.8 3.0 %constant_dynamic-slice_fusion.1 = (bf16[4,1,256,2,256]{4,3,2,1,0:T(2,128)(2,1)S(1)}, bf16[4,1,256,2,256]{4,3,2,1,0:T(2,128)(2,1)S(1)}) fusion(bf16[4,2,256,2,256]{4,3,2,1,0:T(2,128)(2,1)} %bitcast.180, s32[]{:T(128)S(6)} %select_n.117, s32[]{:T(128)S(6)} %select_n.110), kind=kLoop, calls=%fused_computation.159 | loop fusion | bytes 4194312 | tf_op jit(solution)/shard_map/jit(dynamic_index_in_dim)/dynamic_slice | solution.py:219
  162.1 3.4 %fusion.6 = f32[32,40,2,256]{3,1,2,0:T(8,128)S(1)} fusion(bf16[1024,2,256,1]{2,0,1,3:T(8,128)(2,1)S(1)} %bitcast.185, bf16[32,40,1024]{2,1,0:T(8,128)(2,1)} %all_to_all.10), kind=kOutput, calls=%fused_computation.16 | convolution fusion | flops 1342177280 | bytes 6291456 | tf_op jit(solution)/shard_map/scw,wgu->scgu/dot_general | solution.py:222
  165.5 3.4 %fusion.12 = f32[32,40,2,256]{3,1,2,0:T(8,128)S(1)} fusion(f32[32,40,2,256]{3,1,2,0:T(8,128)S(1)} %fusion.6, bf16[1024,2,256,1]{2,0,1,3:T(8,128)(2,1)S(1)} %bitcast.184, bf16[32,40,1024]{2,1,0:T(8,128)(2,1)} %collective-permute-done.9), kind=kOutput, calls=%fused_computation.28 | convolution fusion | flops 1342832640 | bytes 8912896 | tf_op jit(solution)/shard_map/scw,wgu->scgu/dot_general | solution.py:224
  170.8 2.0 copy-done.3
  173.3 4.7 %collective-permute-done.10 = bf16[32,40,1024]{2,1,0:T(8,128)(2,1)} collective-permute-done((bf16[32,40,1024]{2,1,0:T(8,128)(2,1)S(1)}, bf16[32,40,1024]{2,1,0:T(8,128)(2,1)}, u32[]{:S(2)}, u32[]{:S(2)}) %collective-permute-start.10) | collective-permute-done | bytes 2621472 | tf_op jit(solution)/shard_map/ppermute | solution.py:241
  178.0 3.7 %convert_add_fusion = f32[32,40,1024]{2,1,0:T(8,128)S(1)} fusion(bf16[32,40,1024]{2,1,0:T(8,128)(2,1)} %collective-permute-done.10, bf16[32,40,2048]{2,1,0:T(8,128)(2,1)} %copy-done.3, s32[]{:T(128)S(6)} %select_n.130), kind=kLoop, calls=%fused_computation.6 | loop fusion | flops 3932160 | bytes 10485764 | tf_op jit(solution)/shard_map/add | solution.py:241
  181.7 2.3 copy-done.2
  185.7 29.7 %collective-permute-done.11 = bf16[32,40,512]{2,1,0:T(8,128)(2,1)S(1)} collective-permute-done((bf16[32,40,512]{2,1,0:T(8,128)(2,1)S(1)}, bf16[32,40,512]{2,1,0:T(8,128)(2,1)S(1)}, u32[]{:S(2)}, u32[]{:S(2)}) %collective-permute-start.11) | collective-permute-done | bytes 1310752 | tf_op jit(solution)/shard_map/ppermute | solution.py:245
  215.4 2.2 add_convert_fusion
  218.8 8.7 %all-to-all-start.1 = ((bf16[64,40,256]{2,1,0:T(8,128)(2,1)}), bf16[64,40,256]{2,1,0:T(8,128)(2,1)}, u32[]{:S(2)}, u32[]{:S(2)}) async-start(bf16[64,40,256]{2,1,0:T(8,128)(2,1)} %bitcast.56), calls=%async_computation.1 | async-start | bytes 2621440 | tf_op jit(solution)/shard_map/all_to_all | solution.py:251
  229.8 33.1 %all-to-all-done.1 = bf16[64,40,256]{2,1,0:T(8,128)(2,1)} async-done(((bf16[64,40,256]{2,1,0:T(8,128)(2,1)}), bf16[64,40,256]{2,1,0:T(8,128)(2,1)}, u32[]{:S(2)}, u32[]{:S(2)}) %all-to-all-start.1) | async-done | bytes 1310752 | tf_op jit(solution)/shard_map/all_to_all | solution.py:251
  262.9 4.5 %fusion.31 = bf16[256,256]{1,0:T(8,128)(2,1)} fusion(bf16[64,40,256]{2,1,0:T(8,128)(2,1)} %all-to-all-done.1, f32[256,64]{0,1:T(8,128)S(1)} %copy-done.10, f32[256,64]{0,1:T(8,128)S(1)} %fusion.59, f32[256,4,256]{2,0,1:T(8,128)} %get-tuple-element.9, s32[]{:T(128)S(6)} %select_n.127), kind=kOutput, calls=%fused_computation.41 | convolution fusion | flops 2014707712 | bytes 1835012 | tf_op jit(solution)/shard_map/dot_general | solution.py:253
  (157 shorter events, 39.2 us)
Async XLA Ops:
  0.6 2.2 copy-start
  2.8 3.0 %copy-start.15 = (s32[4,8]{1,0:T(4,128)S(1)}, s32[4,8]{1,0:T(4,128)}, u32[]{:S(2)}) copy-start(s32[4,8]{1,0:T(4,128)} %param.17) | copy-start | bytes 388
  2.8 3.3 %copy-start.18 = (s32[4,64]{1,0:T(4,128)S(1)}, s32[4,64]{1,0:T(4,128)}, u32[]{:S(2)}) copy-start(s32[4,64]{1,0:T(4,128)} %param.19) | copy-start | bytes 3076
  5.5 2.6 copy-start.14
  5.6 7.2 %collective-permute-start = (f32[2,256]{1,0:T(2,128)S(1)}, f32[2,256]{1,0:T(2,128)S(1)}, u32[]{:S(2)}, u32[]{:S(2)}) collective-permute-start(f32[2,256]{1,0:T(2,128)S(1)} %pad_maximum_fusion.3), channel_id=1, source_target_pairs={{0,1},{1,0},{2,3},{3,2},{4,5},{5,4},{6,7},{7,6},{8,9},{9,8},{10,11... | collective-permute-start | bytes 6152 | tf_op jit(solution)/shard_map/ppermute | solution.py:91
  8.3 11.7 %copy-start.16 = (f32[2,256]{1,0:T(2,128)S(1)}, f32[2,256]{1,0:T(2,128)}, u32[]{:S(2)}) copy-start(f32[2,256]{1,0:T(2,128)} %param.23) | copy-start | bytes 6148
  12.9 3.7 %collective-permute-start.1 = (f32[2,256]{1,0:T(2,128)S(1)}, f32[2,256]{1,0:T(2,128)S(1)}, u32[]{:S(2)}, u32[]{:S(2)}) collective-permute-start(f32[2,256]{1,0:T(2,128)S(1)} %fusion.98), channel_id=1, source_target_pairs={{0,2},{2,0},{1,3},{3,1},{4,6},{6,4},{5,7},{7,5},{8,10},{10,8},{9,1... | collective-permute-start | bytes 6152 | tf_op jit(solution)/shard_map/ppermute | solution.py:92
  16.6 5.3 %collective-permute-start.2 = (f32[2,256]{1,0:T(2,128)S(1)}, f32[2,256]{1,0:T(2,128)S(1)}, u32[]{:S(2)}, u32[]{:S(2)}) collective-permute-start(f32[2,256]{1,0:T(2,128)S(1)} %fusion.135), channel_id=1, source_target_pairs={{0,4},{4,0},{1,5},{5,1},{2,6},{6,2},{3,7},{7,3},{8,12},{12,8},{9,1... | collective-permute-start | bytes 6152 | tf_op jit(solution)/shard_map/ppermute | solution.py:93
  26.0 1.6 copy-start.6
  28.6 1.6 copy-start.7
  35.0 1.9 copy-start.11
  35.1 1.9 copy-start.12
  37.0 2.3 collective-permute-start.3
  37.7 6.2 %copy-start.4 = (bf16[256,2048]{1,0:T(8,128)(2,1)S(1)}, bf16[256,2048]{1,0:T(8,128)(2,1)}, u32[]{:S(2)}) copy-start(bf16[256,2048]{1,0:T(8,128)(2,1)} %param.15) | copy-start | bytes 3145732
  40.5 2.8 %copy-start.5 = (f32[256,4,256]{2,0,1:T(8,128)}, f32[256,4,256]{2,0,1:T(8,128)S(1)}, u32[]{:S(2)}) copy-start(f32[256,4,256]{2,0,1:T(8,128)S(1)} %bitcast_add_fusion.1) | copy-start | bytes 3145732
  40.5 5.6 %copy-start.13 = (f32[2048]{0:T(1024)S(1)}, f32[2048]{0:T(1024)}, u32[]{:S(2)}) copy-start(f32[2048]{0:T(1024)} %param.25) | copy-start | bytes 24580
  41.3 8.9 %collective-permute-start.4 = (bf16[256,2,256]{2,0,1:T(8,128)(2,1)}, bf16[256,2,256]{2,0,1:T(8,128)(2,1)}, u32[]{:S(2)}, u32[]{:S(2)}) collective-permute-start(bf16[256,2,256]{2,0,1:T(8,128)(2,1)} %fusion.58), channel_id=1, source_target_pairs={{0,2},{2,0},{1,3},{3,1},{4,6},{6,4},{5,7},{7,5},{8,10},{10,8},{9,1... | collective-permute-start | bytes 786440 | tf_op jit(solution)/shard_map/ppermute | solution.py:157
  43.9 2.2 copy-start.9
  51.4 6.7 %collective-permute-start.5 = (bf16[256,256]{1,0:T(8,128)(2,1)S(1)}, bf16[256,256]{1,0:T(8,128)(2,1)S(1)}, u32[]{:S(2)}, u32[]{:S(2)}) collective-permute-start(bf16[256,256]{1,0:T(8,128)(2,1)S(1)} %fusion.60), channel_id=1, source_target_pairs={{0,4},{4,0},{1,5},{5,1},{2,6},{6,2},{3,7},{7,3},{8,12},{12,8},{9,1... | collective-permute-start | bytes 393224 | tf_op jit(solution)/shard_map/ppermute | solution.py:162
  58.2 6.6 %collective-permute-start.6 = (bf16[256,256]{1,0:T(8,128)(2,1)S(1)}, bf16[256,256]{1,0:T(8,128)(2,1)S(1)}, u32[]{:S(2)}, u32[]{:S(2)}) collective-permute-start(bf16[256,256]{1,0:T(8,128)(2,1)S(1)} %get-tuple-element.21), channel_id=1, source_target_pairs={{0,4},{4,0},{1,5},{5,1},{2,6},{6,2},{3,7},{7,3},{8,12},{12,8},{9,1... | collective-permute-start | bytes 393224 | tf_op jit(solution)/shard_map/ppermute | solution.py:167
  64.8 6.5 %collective-permute-start.7 = (bf16[256,2,256]{2,0,1:T(8,128)(2,1)S(1)}, bf16[256,2,256]{2,0,1:T(8,128)(2,1)S(1)}, u32[]{:S(2)}, u32[]{:S(2)}) collective-permute-start(bf16[256,2,256]{2,0,1:T(8,128)(2,1)S(1)} %fusion.55), channel_id=1, source_target_pairs={{0,2},{2,0},{1,3},{3,1},{4,6},{6,4},{5,7},{7,5},{8,10},{10,8},{9,1... | collective-permute-start | bytes 786440 | tf_op jit(solution)/shard_map/ppermute | solution.py:173
  72.8 3.9 %collective-permute-start.8 = (f32[256]{0:T(256)S(1)}, f32[256]{0:T(256)}, u32[]{:S(2)}, u32[]{:S(2)}) collective-permute-start(f32[256]{0:T(256)S(1)} %get-tuple-element.8), channel_id=1, source_target_pairs={{0,1},{1,0},{2,3},{3,2},{4,5},{5,4},{6,7},{7,6},{8,9},{9,8},{10,11... | collective-permute-start | bytes 3080 | tf_op jit(solution)/shard_map/ppermute | solution.py:181
  153.6 11.9 %collective-permute-start.9 = (bf16[32,40,1024]{2,1,0:T(8,128)(2,1)}, bf16[32,40,1024]{2,1,0:T(8,128)(2,1)}, u32[]{:S(2)}, u32[]{:S(2)}) collective-permute-start(bf16[32,40,1024]{2,1,0:T(8,128)(2,1)} %all_to_all.10), channel_id=1, source_target_pairs={{0,1},{1,0},{2,3},{3,2},{4,5},{5,4},{6,7},{7,6},{8,9},{9,8},{10,11... | collective-permute-start | bytes 7864328 | tf_op jit(solution)/shard_map/ppermute | solution.py:214
  162.1 3.4 %copy-start.8 = (bf16[4,1,256,2,256]{4,2,0,3,1:T(8,128)(2,1)S(1)}, bf16[4,1,256,2,256]{4,2,0,3,1:T(8,128)(2,1)}, u32[]{:S(2)}) copy-start(bf16[4,1,256,2,256]{4,2,0,3,1:T(8,128)(2,1)} %copy.146) | copy-start | bytes 3145732
  170.5 2.3 copy-start.3
  172.8 5.2 %collective-permute-start.10 = (bf16[32,40,1024]{2,1,0:T(8,128)(2,1)S(1)}, bf16[32,40,1024]{2,1,0:T(8,128)(2,1)}, u32[]{:S(2)}, u32[]{:S(2)}) collective-permute-start(bf16[32,40,1024]{2,1,0:T(8,128)(2,1)S(1)} %constant_dynamic-slice_fusion), channel_id=1, source_target_pairs={{0,1},{1,0},{2,3},{3,2},{4,5},{5,4},{6,7},{7,6},{8,9},{9,8},{10,11... | collective-permute-start | bytes 7864328 | tf_op jit(solution)/shard_map/ppermute | solution.py:241
  181.7 2.3 copy-start.2
  184.2 31.1 %collective-permute-start.11 = (bf16[32,40,512]{2,1,0:T(8,128)(2,1)S(1)}, bf16[32,40,512]{2,1,0:T(8,128)(2,1)S(1)}, u32[]{:S(2)}, u32[]{:S(2)}) collective-permute-start(bf16[32,40,512]{2,1,0:T(8,128)(2,1)S(1)} %dynamic-slice_convert_fusion), channel_id=1, source_target_pairs={{0,2},{2,0},{1,3},{3,1},{4,6},{6,4},{5,7},{7,5},{8,10},{10,8},{9,1... | collective-permute-start | bytes 3932168 | tf_op jit(solution)/shard_map/ppermute | solution.py:245
  217.6 10.0 %copy-start.17 = (s32[4,8]{1,0:T(4,128)S(1)}, s32[4,8]{1,0:T(4,128)}, u32[]{:S(2)}) copy-start(s32[4,8]{1,0:T(4,128)} %param.20) | copy-start | bytes 388
  217.7 45.3 %copy-start.10 = (f32[256,64]{0,1:T(8,128)S(1)}, f32[256,64]{0,1:T(8,128)}, u32[]{:S(2)}) copy-start(f32[256,64]{0,1:T(8,128)} %get-tuple-element.4) | copy-start | bytes 196612
  218.8 44.1 %all-to-all-start.1 = ((bf16[64,40,256]{2,1,0:T(8,128)(2,1)}), bf16[64,40,256]{2,1,0:T(8,128)(2,1)}, u32[]{:S(2)}, u32[]{:S(2)}) async-start(bf16[64,40,256]{2,1,0:T(8,128)(2,1)} %bitcast.56), calls=%async_computation.1 | async-start | bytes 2621440 | tf_op jit(solution)/shard_map/all_to_all | solution.py:251
  262.9 4.5 %copy-start.1 = (bf16[2048,3,256]{2,0,1:T(8,128)(2,1)S(1)}, bf16[2048,3,256]{2,0,1:T(8,128)(2,1)}, u32[]{:S(2)}) copy-start(bf16[2048,3,256]{2,0,1:T(8,128)(2,1)} %param.22) | copy-start | bytes 9437188
